TPU v7x, 32 devices: a whole 2x2x4 slice. The times are simulated.
32 devices in a mesh: grp: 8 (over z, x), rep: 4 (over y, core).
Axes of the slice: x: 2, y: 2, z: 4, core: 2. Of those that a mesh axis runs over, the one named last changes fastest.
Arguments:
- three_center: bfloat16 [4, 64, 32, 6, 4096], P('rep', 'grp'), may hold values from -2 to 2
- metric: bfloat16 [4, 64, 64], P('rep'), may hold values from -0.75 to 0.75
- occupied: bfloat16 [2048, 48], replicated, may hold values from -0.3125 to 0.3125
- nu_list: int32 [32, 6], replicated, may hold values from 0 to 31, as said below
- nu_count: int32 [32], replicated, may hold values from 1 to 6
- block_size: int32 [32], replicated, may hold values from 32 to 64
Outputs:
- exchange_matrix: float32 [2048, 2048], P('rep', 'grp')
Inputs may be any that keep to these rules, and one draw needn't show every extreme that they name: `nu_list`: entry 0 of row m is m itself; the other entries of a row are distinct blocks other than m.
All inputs are finite; a program needn't handle non-finite values.
Results may differ from a plain program's by a relative error of at most 0.0024.
Values may be sent and summed in bfloat16 or wider, within the bound.
No kernel may reach another device: no remote copies, remote signals or barrier semaphores. Data moves between devices by JAX's collectives and lax.ppermute only.
A program may use at most 192 MiB of HBM per device.

v0:
```python
import jax
import jax.numpy as jnp
from jax import lax
from jax.sharding import PartitionSpec as P

NB = 64
N_CHUNKS = 4


def body(three_center, metric, occupied, nu_list, nu_count, block_size):
    n_mu, knu = nu_list.shape
    n_occ = occupied.shape[1]
    aux_dev = three_center.shape[1]
    occ_c = n_occ // N_CHUNKS
    lanes = jnp.arange(NB, dtype=jnp.int32)
    row_live = lanes[None, :] < block_size[:, None]
    col_live = lanes[None, None, :] < block_size[nu_list][:, :, None]
    slot_live = jnp.arange(knu, dtype=jnp.int32)[None, :] < nu_count[:, None]
    mask = row_live[:, None, :, None] & col_live[:, :, None, :] & slot_live[:, :, None, None]
    blocks = three_center[0].reshape(aux_dev, n_mu, knu, NB, NB)
    masked = jnp.where(mask[None], blocks, jnp.zeros((), jnp.bfloat16))
    picked = occupied.reshape(n_mu, NB, N_CHUNKS, occ_c)[nu_list]
    half = jnp.einsum(
        "qmkab,mkbci->cqmai", masked, picked, preferred_element_type=jnp.float32
    ).astype(jnp.bfloat16)
    half = half.reshape(N_CHUNKS, aux_dev, n_mu, NB * occ_c)
    n_grp = lax.axis_size("grp")
    rows = n_mu * NB // n_grp
    start = lax.axis_index("grp") * rows
    term = None
    for c in range(N_CHUNKS):
        gathered = lax.all_gather(half[c], "grp", axis=0, tiled=True)
        n_aux = gathered.shape[0]
        gathered = gathered.reshape(n_aux, n_mu, NB, occ_c)
        orbital = jnp.einsum(
            "pq,qmai->mapi", metric[0], gathered, preferred_element_type=jnp.float32
        ).astype(jnp.bfloat16)
        orbital = orbital.reshape(n_mu * NB, n_aux * occ_c)
        mine = lax.dynamic_slice_in_dim(orbital, start, rows, axis=0)
        part = jnp.dot(orbital, mine.T, preferred_element_type=jnp.float32)
        term = part if term is None else term + part
    return lax.psum_scatter(term, "rep", scatter_dimension=0, tiled=True)


def solution(mesh):
    return jax.shard_map(
        body,
        mesh=mesh,
        in_specs=(P("rep", "grp", None, None, None), P("rep", None, None), P(), P(), P(), P()),
        out_specs=P("rep", "grp"),
        check_vma=False,
    )
```

profile of v0, /device:TPU:0, one launch (start us, length us, event | category | flops | bytes accessed | tf_op | source)
XLA Modules:
  0.0 872.6 jit_solution(10821817166071291102)
XLA Ops:
  6.6 34.4 %reshape_squeeze.3 = bf16[8,32,6,64,64]{4,3,1,2,0:T(8,128)(2,1)} reshape(bf16[1,8,32,6,4096]{4,2,3,1,0:T(8,128)(2,1)} %param.6) | data formatting | bytes 25165824 | tf_op jit(solution)/shard_map/reshape;squeeze | solution.py:20
  43.9 2.6 gather_fusion
  48.1 17.4 %fusion.4 = bf16[4,8,32,64,12]{3,4,1,0,2:T(8,128)(2,1)} fusion(bf16[8,32,6,64,64]{4,3,1,2,0:T(8,128)(2,1)} %reshape_squeeze.3, pred[32,6,64,64]{3,2,1,0:T(8,128)(4,1)S(1)} %and_and_fusion, bf16[32,6,64,4,12,1]{2,3,4,1,0,5:T(4,128)(2,1)S(1)} %bitcast.76), kind=kOutput, calls=%fused_computation.13 | convolution fusion | flops 611057664 | bytes 16121856 | tf_op jit(solution)/shard_map/qmkab,mkbci->cqmai/dot_general | solution.py:23
  65.4 4.3 fusion.22
  69.8 5.3 copy.31
  75.1 4.1 copy.35
  79.2 10.4 %all-gather.9.cloned.1.call-start = ((), (), s32[]{:S(2)}) async-start(), calls=%async_computation.3 | async-start | bytes 14155776 | tf_op jit(solution)/shard_map/all_gather | solution.py:32
  89.7 4.1 copy.39
  93.9 4.1 copy.43
  98.1 156.4 %all-gather.5.cloned.1.call-done = bf16[64,32,768]{1,0,2:T(8,128)(2,1)} async-done(((bf16[8,32,768]{1,0,2:T(8,128)(2,1)}), bf16[64,32,768]{1,0,2:T(8,128)(2,1)}) %all-gather.5.cloned.1.call-update) | async-done | bytes 3145744 | tf_op jit(solution)/shard_map/all_gather | solution.py:32
  254.5 15.7 %copy.33 = bf16[64,32,64,12]{0,2,3,1:T(8,128)(2,1)} copy(bf16[64,32,64,12]{1,0,3,2:T(8,128)(2,1)} %bitcast.77) | data formatting | bytes 6291456 | tf_op jit(solution)/shard_map/reshape | solution.py:34
  270.3 7.2 convert_bitcast_fusion.3
  277.5 9.4 %copy.34 = bf16[32,64,64,12]{1,0,3,2:T(8,128)(2,1)} copy(bf16[32,64,64,12]{2,1,3,0:T(8,128)(2,1)} %convert_bitcast_fusion.3) | data formatting | bytes 6291456 | tf_op jit(solution)/shard_map/convert_element_type | solution.py:37
  286.9 9.7 %reshape.85 = bf16[2048,768]{0,1:T(8,128)(2,1)} reshape(bf16[32,64,64,12]{1,0,3,2:T(8,128)(2,1)} %copy.34) | data formatting | bytes 6291456 | tf_op jit(solution)/shard_map/reshape | solution.py:38
  296.6 134.7 %all-gather.7.cloned.1.call-done = bf16[64,32,768]{1,0,2:T(8,128)(2,1)} async-done(((bf16[8,32,768]{1,0,2:T(8,128)(2,1)}), bf16[64,32,768]{1,0,2:T(8,128)(2,1)}) %all-gather.7.cloned.1.call-update) | async-done | bytes 3145744 | tf_op jit(solution)/shard_map/all_gather | solution.py:32
  431.4 15.8 %copy.37 = bf16[64,32,64,12]{0,2,3,1:T(8,128)(2,1)} copy(bf16[64,32,64,12]{1,0,3,2:T(8,128)(2,1)} %bitcast.78) | data formatting | bytes 6291456 | tf_op jit(solution)/shard_map/reshape | solution.py:34
  447.1 7.3 convert_bitcast_fusion.2
  454.4 9.4 %copy.38 = bf16[32,64,64,12]{1,0,3,2:T(8,128)(2,1)} copy(bf16[32,64,64,12]{2,1,3,0:T(8,128)(2,1)} %convert_bitcast_fusion.2) | data formatting | bytes 6291456 | tf_op jit(solution)/shard_map/convert_element_type | solution.py:37
  463.8 8.5 reshape.87
  472.3 135.9 %all-gather.9.cloned.1.call-done = bf16[64,32,768]{1,0,2:T(8,128)(2,1)} async-done(((bf16[8,32,768]{1,0,2:T(8,128)(2,1)}), bf16[64,32,768]{1,0,2:T(8,128)(2,1)}) %all-gather.9.cloned.1.call-update) | async-done | bytes 3145744 | tf_op jit(solution)/shard_map/all_gather | solution.py:32
  608.2 15.8 %copy.41 = bf16[64,32,64,12]{0,2,3,1:T(8,128)(2,1)} copy(bf16[64,32,64,12]{1,0,3,2:T(8,128)(2,1)} %bitcast.79) | data formatting | bytes 6291456 | tf_op jit(solution)/shard_map/reshape | solution.py:34
  624.0 7.2 convert_bitcast_fusion.1
  631.1 9.5 %copy.42 = bf16[32,64,64,12]{1,0,3,2:T(8,128)(2,1)} copy(bf16[32,64,64,12]{2,1,3,0:T(8,128)(2,1)} %convert_bitcast_fusion.1) | data formatting | bytes 6291456 | tf_op jit(solution)/shard_map/convert_element_type | solution.py:37
  640.6 9.7 %reshape.89 = bf16[2048,768]{0,1:T(8,128)(2,1)} reshape(bf16[32,64,64,12]{1,0,3,2:T(8,128)(2,1)} %copy.42) | data formatting | bytes 6291456 | tf_op jit(solution)/shard_map/reshape | solution.py:38
  650.4 134.5 %all-gather.11.cloned.1.call-done = bf16[64,32,768]{1,0,2:T(8,128)(2,1)} async-done(((bf16[8,32,768]{1,0,2:T(8,128)(2,1)}), bf16[64,32,768]{1,0,2:T(8,128)(2,1)}) %all-gather.11.cloned.1.call-update) | async-done | bytes 3145744 | tf_op jit(solution)/shard_map/all_gather | solution.py:32
  784.9 15.5 %copy.45 = bf16[64,32,64,12]{0,2,3,1:T(8,128)(2,1)} copy(bf16[64,32,64,12]{1,0,3,2:T(8,128)(2,1)} %bitcast.80) | data formatting | bytes 6291456 | tf_op jit(solution)/shard_map/reshape | solution.py:34
  800.3 7.2 convert_bitcast_fusion
  807.6 9.4 %copy.46 = bf16[32,64,64,12]{1,0,3,2:T(8,128)(2,1)} copy(bf16[32,64,64,12]{2,1,3,0:T(8,128)(2,1)} %convert_bitcast_fusion) | data formatting | bytes 6291456 | tf_op jit(solution)/shard_map/convert_element_type | solution.py:37
  817.0 9.7 %reshape.91 = bf16[2048,768]{0,1:T(8,128)(2,1)} reshape(bf16[32,64,64,12]{1,0,3,2:T(8,128)(2,1)} %copy.46) | data formatting | bytes 6291456 | tf_op jit(solution)/shard_map/reshape | solution.py:38
  826.7 3.0 fusion.11
  833.5 2.5 convolution_add_fusion
  836.0 29.8 %reduce-scatter.2.cloned.1.call-done = f32[512,256]{1,0:T(8,128)} async-done(((f32[2048,256]{1,0:T(8,128)}), f32[512,256]{1,0:T(8,128)}) %reduce-scatter.2.cloned.1.call-update) | async-done | bytes 524304 | tf_op jit(solution)/shard_map/reduce_scatter | solution.py:42
  (37 shorter events, 8.4 us)
Async XLA Ops:
  6.5 263.7 %copy-start = (bf16[1,64,64]{2,1,0:T(8,128)(2,1)S(1)}, bf16[1,64,64]{2,1,0:T(8,128)(2,1)}, u32[]{:S(2)}) copy-start(bf16[1,64,64]{2,1,0:T(8,128)(2,1)} %param.7) | copy-start | bytes 24580
  6.5 34.5 %copy-start.6 = (s32[32]{0:T(128)S(1)}, s32[32]{0:T(128)}, u32[]{:S(2)}) copy-start(s32[32]{0:T(128)} %param.10) | copy-start | bytes 388
  6.5 34.5 %copy-start.5 = (s32[32,6]{0,1:T(8,128)S(1)}, s32[32,6]{0,1:T(8,128)}, u32[]{:S(2)}) copy-start(s32[32,6]{0,1:T(8,128)} %param.9) | copy-start | bytes 2308
  6.5 34.8 %copy-start.1 = (s32[32]{0:T(128)S(1)}, s32[32]{0:T(128)}, u32[]{:S(2)}) copy-start(s32[32]{0:T(128)} %param.11) | copy-start | bytes 388
  6.5 248.0 %all-gather.5.cloned.1.call-start = ((), (), s32[]{:S(2)}) async-start(), calls=%async_computation.1 | async-start | bytes 14155776 | tf_op jit(solution)/shard_map/all_gather | solution.py:32
  41.4 1.8 copy-start.4
  75.1 356.3 %all-gather.7.cloned.1.call-start = ((), (), s32[]{:S(2)}) async-start(), calls=%async_computation.2 | async-start | bytes 14155776 | tf_op jit(solution)/shard_map/all_gather | solution.py:32
  79.2 528.9 %all-gather.9.cloned.1.call-start = ((), (), s32[]{:S(2)}) async-start(), calls=%async_computation.3 | async-start | bytes 14155776 | tf_op jit(solution)/shard_map/all_gather | solution.py:32
  93.8 691.1 %all-gather.11.cloned.1.call-start = ((), (), s32[]{:S(2)}) async-start(), calls=%async_computation.4 | async-start | bytes 14155776 | tf_op jit(solution)/shard_map/all_gather | solution.py:32
  98.0 767.7 %reduce-scatter.2.cloned.1.call-start = ((), (), s32[]{:S(2)}) async-start(), calls=%async_computation.5 | async-start | bytes 2621440 | tf_op jit(solution)/shard_map/reduce_scatter | solution.py:42
  829.7 1.9 copy-start.2
  831.6 1.9 copy-start.3
Sparse Core Ops, SparseCore 0:
  75.2 179.2 all-gather.4
  256.6 174.7 all-gather.6
  433.4 174.7 all-gather.8
  610.1 174.7 all-gather.10
  836.1 29.6 reduce-scatter.1
where the time goes:
time: 885 us; the launch traced here: 873 us
  waiting for transfers between devices  591 us (67%)
  local copies, waits for them, and re-layouts  201 us (23%)
  matrix products  53.9 us (6%)
  between operations  13.7 us (2%)
  starting transfers between devices  10.6 us (1%)
    all_gather x4, waiting for transfers between devices, body(): gathered = lax.all_gather(half[c], 'grp', axis=0, tiled=True)  562 us
    reshape x4, local copies, waits for them, and re-layouts, body(): gathered = gathered.reshape(n_aux, n_mu, NB, occ_c)  62.7 us
    reshape x4, local copies, waits for them, and re-layouts, body(): orbital = orbital.reshape(n_mu * NB, n_aux * occ_c)  37.7 us
    convert_element_type x4, local copies, waits for them, and re-layouts, body(): orbital = jnp.einsum('pq,qmai->mapi', metric[0], gathered, preferred_elem...  37.7 us
    another operation x1, local copies, waits for them, and re-layouts, body(): blocks = three_center[0].reshape(aux_dev, n_mu, knu, NB, NB)  34.4 us
    reduce_scatter x1, waiting for transfers between devices, body(): return lax.psum_scatter(term, 'rep', scatter_dimension=0, tiled=True)  29.8 us
    dot_general x4, matrix products, body(): jnp.einsum('pq,qmai->mapi', metric[0], gathered, preferred_element_type=j...  28.9 us
    slice x5, local copies, waits for them, and re-layouts, body(): gathered = lax.all_gather(half[c], 'grp', axis=0, tiled=True)  22 us
  transfers between devices with their start and end apart: 5, of which 5 were waited for; matrix products, arithmetic and copies ran while one was open for 16% of the time, Pallas kernels for 0%

commit v1 on v0

--- a/solution.py
+++ b/solution.py
@@ -29,7 +29,15 @@
     start = lax.axis_index("grp") * rows
     term = None
     for c in range(N_CHUNKS):
-        gathered = lax.all_gather(half[c], "grp", axis=0, tiled=True)
+        x = half[c]
+        count = lax.axis_size("grp")
+        right = [(i, (i + 1) % count) for i in range(count)]
+        shards = [x]
+        for far in range(1, count):
+            shards = [lax.ppermute(shards[0], "grp", right), *shards]
+        whole = jnp.concatenate(shards, axis=0)
+        places = (lax.axis_index("grp") + 1) * shards[-1].shape[0]
+        gathered = jnp.roll(whole, places, axis=0)
         n_aux = gathered.shape[0]
         gathered = gathered.reshape(n_aux, n_mu, NB, occ_c)
         orbital = jnp.einsum(

time: 885 us -> 573 us (0.65)
  waiting for transfers between devices: 591 us -> 239 us
  matrix products: 53.9 us -> 76.4 us
  other arithmetic: 1.82 us -> 13.4 us
    all_gather x4 -> x0, waiting for transfers between devices: 562 us -> none  [body(): gathered = lax.all_gather(half[c], 'grp', axis=0, tiled=True)]
    ppermute x0 -> x28, waiting for transfers between devices: none -> 209 us  [body(): shards = [lax.ppermute(shards[0], 'grp', right), *shards]]
    reshape x4 -> x0, local copies, waits for them, and re-layouts: 62.7 us -> none  [body(): gathered = gathered.reshape(n_aux, n_mu, NB, occ_c)]
    unnamed x14 -> x78, local copies, waits for them, and re-layouts: 1.61 us -> 62.8 us
    dot_general x4, matrix products: 28.9 us -> 51.2 us  [body(): jnp.einsum('pq,qmai->mapi', metric[0], gathered, preferred_element_type=j...]
    ppermute x0 -> x28, starting transfers between devices: none -> 11.2 us  [body(): shards = [lax.ppermute(shards[0], 'grp', right), *shards]]
    all_gather x4 -> x0, starting transfers between devices: 10.5 us -> none  [body(): gathered = lax.all_gather(half[c], 'grp', axis=0, tiled=True)]
    concatenate x0 -> x2, other arithmetic: none -> 9.54 us  [body(): gathered = jnp.roll(whole, places, axis=0)]
  transfers between devices with their start and end apart: 5 -> 29, of which waited for: 5 -> 25; matrix products, arithmetic and copies ran while one was open for 16% -> 5% of each run, Pallas kernels for 0% -> 0%
where the time goes in v1:
time: 573 us; the launch traced here: 562 us
  waiting for transfers between devices  239 us (42%)
  local copies, waits for them, and re-layouts  207 us (36%)
  matrix products  76.4 us (13%)
  between operations  14.3 us (2%)
  other arithmetic  13.4 us (2%)
  starting transfers between devices  11.2 us (2%)
    ppermute x28, waiting for transfers between devices, body(): shards = [lax.ppermute(shards[0], 'grp', right), *shards]  209 us
    unnamed x78, local copies, waits for them, and re-layouts  62.8 us
    dot_general x4, matrix products, body(): jnp.einsum('pq,qmai->mapi', metric[0], gathered, preferred_element_type=j...  51.2 us
    reshape x4, local copies, waits for them, and re-layouts, body(): orbital = orbital.reshape(n_mu * NB, n_aux * occ_c)  38.2 us
    convert_element_type x4, local copies, waits for them, and re-layouts, body(): orbital = jnp.einsum('pq,qmai->mapi', metric[0], gathered, preferred_elem...  38.1 us
    another operation x1, local copies, waits for them, and re-layouts, body(): blocks = three_center[0].reshape(aux_dev, n_mu, knu, NB, NB)  34.4 us
    reduce_scatter x1, waiting for transfers between devices, body(): return lax.psum_scatter(term, 'rep', scatter_dimension=0, tiled=True)  30.1 us
    slice x5, local copies, waits for them, and re-layouts, body(): x = half[c]  23.2 us
  transfers between devices with their start and end apart: 29, of which 25 were waited for; matrix products, arithmetic and copies ran while one was open for 5% of the time, Pallas kernels for 0%

profile of v1, /device:TPU:0, one launch (start us, length us, event | category | flops | bytes accessed | tf_op | source)
XLA Modules:
  0.0 561.7 jit_solution(14481433671691483533)
XLA Ops:
  14.1 34.4 %reshape_squeeze.3 = bf16[8,32,6,64,64]{4,3,1,2,0:T(8,128)(2,1)} reshape(bf16[1,8,32,6,4096]{4,2,3,1,0:T(8,128)(2,1)} %param.8) | data formatting | bytes 25165824 | tf_op jit(solution)/shard_map/reshape;squeeze | solution.py:20
  50.0 17.4 %fusion.12 = bf16[4,8,32,64,12]{3,4,1,0,2:T(8,128)(2,1)} fusion(bf16[8,32,6,64,64]{4,3,1,2,0:T(8,128)(2,1)} %reshape_squeeze.3, pred[32,6,64,64]{3,2,1,0:T(8,128)(4,1)S(1)} %and_and_fusion, bf16[32,6,64,4,12,1]{2,3,4,1,0,5:T(4,128)(2,1)S(1)} %bitcast.72), kind=kOutput, calls=%fused_computation.29 | convolution fusion | flops 611057664 | bytes 16121856 | tf_op jit(solution)/shard_map/qmkab,mkbci->cqmai/dot_general | solution.py:23
  120.4 8.4 %collective-permute-done.1 = bf16[8,32,768]{2,1,0:T(8,128)(2,1)S(1)} collective-permute-done((bf16[8,32,768]{2,1,0:T(8,128)(2,1)}, bf16[8,32,768]{2,1,0:T(8,128)(2,1)S(1)}, u32[]{:S(2)}, u32[]{:S(2)}) %collective-permute-start.1) | collective-permute-done | bytes 393248 | tf_op jit(solution)/shard_map/ppermute | solution.py:37
  128.9 8.4 %collective-permute-done.22 = bf16[8,32,768]{2,1,0:T(8,128)(2,1)S(1)} collective-permute-done((bf16[8,32,768]{2,1,0:T(8,128)(2,1)}, bf16[8,32,768]{2,1,0:T(8,128)(2,1)S(1)}, u32[]{:S(2)}, u32[]{:S(2)}) %collective-permute-start.22) | collective-permute-done | bytes 393248 | tf_op jit(solution)/shard_map/ppermute | solution.py:37
  137.3 8.4 %collective-permute-done.15 = bf16[8,32,768]{2,1,0:T(8,128)(2,1)S(1)} collective-permute-done((bf16[8,32,768]{2,1,0:T(8,128)(2,1)}, bf16[8,32,768]{2,1,0:T(8,128)(2,1)S(1)}, u32[]{:S(2)}, u32[]{:S(2)}) %collective-permute-start.15) | collective-permute-done | bytes 393248 | tf_op jit(solution)/shard_map/ppermute | solution.py:37
  145.7 8.4 %collective-permute-done.8 = bf16[8,32,768]{2,1,0:T(8,128)(2,1)S(1)} collective-permute-done((bf16[8,32,768]{2,1,0:T(8,128)(2,1)S(1)}, bf16[8,32,768]{2,1,0:T(8,128)(2,1)S(1)}, u32[]{:S(2)}, u32[]{:S(2)}) %collective-permute-start.8) | collective-permute-done | bytes 393248 | tf_op jit(solution)/shard_map/ppermute | solution.py:37
  171.0 8.4 %collective-permute-done.16 = bf16[8,32,768]{2,1,0:T(8,128)(2,1)S(1)} collective-permute-done((bf16[8,32,768]{2,1,0:T(8,128)(2,1)S(1)}, bf16[8,32,768]{2,1,0:T(8,128)(2,1)S(1)}, u32[]{:S(2)}, u32[]{:S(2)}) %collective-permute-start.16) | collective-permute-done | bytes 393248 | tf_op jit(solution)/shard_map/ppermute | solution.py:37
  179.4 8.4 %collective-permute-done.9 = bf16[8,32,768]{2,1,0:T(8,128)(2,1)S(1)} collective-permute-done((bf16[8,32,768]{2,1,0:T(8,128)(2,1)S(1)}, bf16[8,32,768]{2,1,0:T(8,128)(2,1)S(1)}, u32[]{:S(2)}, u32[]{:S(2)}) %collective-permute-start.9) | collective-permute-done | bytes 393248 | tf_op jit(solution)/shard_map/ppermute | solution.py:37
  204.7 8.4 %collective-permute-done.17 = bf16[8,32,768]{2,1,0:T(8,128)(2,1)S(1)} collective-permute-done((bf16[8,32,768]{2,1,0:T(8,128)(2,1)S(1)}, bf16[8,32,768]{2,1,0:T(8,128)(2,1)S(1)}, u32[]{:S(2)}, u32[]{:S(2)}) %collective-permute-start.17) | collective-permute-done | bytes 393248 | tf_op jit(solution)/shard_map/ppermute | solution.py:37
  221.5 8.4 %collective-permute-done.4 = bf16[8,32,768]{2,1,0:T(8,128)(2,1)S(1)} collective-permute-done((bf16[8,32,768]{2,1,0:T(8,128)(2,1)S(1)}, bf16[8,32,768]{2,1,0:T(8,128)(2,1)S(1)}, u32[]{:S(2)}, u32[]{:S(2)}) %collective-permute-start.4) | collective-permute-done | bytes 393248 | tf_op jit(solution)/shard_map/ppermute | solution.py:37
  230.0 8.5 %collective-permute-done.25 = bf16[8,32,768]{2,1,0:T(8,128)(2,1)} collective-permute-done((bf16[8,32,768]{2,1,0:T(8,128)(2,1)S(1)}, bf16[8,32,768]{2,1,0:T(8,128)(2,1)}, u32[]{:S(2)}, u32[]{:S(2)}) %collective-permute-start.25) | collective-permute-done | bytes 393248 | tf_op jit(solution)/shard_map/ppermute | solution.py:37
  272.2 8.4 %collective-permute-done.19 = bf16[8,32,768]{2,1,0:T(8,128)(2,1)} collective-permute-done((bf16[8,32,768]{2,1,0:T(8,128)(2,1)}, bf16[8,32,768]{2,1,0:T(8,128)(2,1)}, u32[]{:S(2)}, u32[]{:S(2)}) %collective-permute-start.19) | collective-permute-done | bytes 393248 | tf_op jit(solution)/shard_map/ppermute | solution.py:37
  280.6 8.4 %collective-permute-done.12 = bf16[8,32,768]{2,1,0:T(8,128)(2,1)} collective-permute-done((bf16[8,32,768]{2,1,0:T(8,128)(2,1)}, bf16[8,32,768]{2,1,0:T(8,128)(2,1)}, u32[]{:S(2)}, u32[]{:S(2)}) %collective-permute-start.12) | collective-permute-done | bytes 393248 | tf_op jit(solution)/shard_map/ppermute | solution.py:37
  289.1 8.4 %collective-permute-done.6 = bf16[8,32,768]{2,1,0:T(8,128)(2,1)} collective-permute-done((bf16[8,32,768]{2,1,0:T(8,128)(2,1)}, bf16[8,32,768]{2,1,0:T(8,128)(2,1)}, u32[]{:S(2)}, u32[]{:S(2)}) %collective-permute-start.6) | collective-permute-done | bytes 393248 | tf_op jit(solution)/shard_map/ppermute | solution.py:37
  303.9 17.9 %collective-permute-done.13 = bf16[8,32,768]{2,1,0:T(8,128)(2,1)S(1)} collective-permute-done((bf16[8,32,768]{2,1,0:T(8,128)(2,1)}, bf16[8,32,768]{2,1,0:T(8,128)(2,1)S(1)}, u32[]{:S(2)}, u32[]{:S(2)}) %collective-permute-start.13) | collective-permute-done | bytes 393248 | tf_op jit(solution)/shard_map/ppermute | solution.py:37
  334.7 11.3 %copy.84 = bf16[64,32,768]{0,1,2:T(8,128)(2,1)} copy(bf16[64,32,768]{2,1,0:T(8,128)(2,1)S(1)} %get-tuple-element.10) | data formatting | bytes 6291456
  346.0 12.8 %convert_bitcast_fusion = bf16[32,64,64,12]{2,1,3,0:T(8,128)(2,1)} fusion(bf16[64,32,64,12]{0,1,3,2:T(8,128)(2,1)} %bitcast.73, bf16[1,64,64]{2,1,0:T(8,128)(2,1)S(1)} %copy-done), kind=kOutput, calls=%fused_computation.24 | convolution fusion | flops 202899456 | bytes 6299648 | tf_op jit(solution)/shard_map/pq,qmai->mapi/dot_general | solution.py:43
  358.8 9.4 %copy.74 = bf16[32,64,64,12]{1,0,3,2:T(8,128)(2,1)} copy(bf16[32,64,64,12]{2,1,3,0:T(8,128)(2,1)} %convert_bitcast_fusion) | data formatting | bytes 6291456 | tf_op jit(solution)/shard_map/convert_element_type | solution.py:45
  368.3 8.7 %reshape.91 = bf16[2048,768]{0,1:T(8,128)(2,1)S(1)} reshape(bf16[32,64,64,12]{1,0,3,2:T(8,128)(2,1)} %copy.74) | data formatting | bytes 6291456 | tf_op jit(solution)/shard_map/reshape | solution.py:46
  382.8 12.2 %copy.82 = bf16[64,32,768]{0,1,2:T(8,128)(2,1)} copy(bf16[64,32,768]{2,1,0:T(8,128)(2,1)} %get-tuple-element.12) | data formatting | bytes 6291456
  395.0 12.8 %convert_bitcast_fusion.2 = bf16[32,64,64,12]{2,1,3,0:T(8,128)(2,1)} fusion(bf16[64,32,64,12]{0,1,3,2:T(8,128)(2,1)} %bitcast.74, bf16[1,64,64]{2,1,0:T(8,128)(2,1)S(1)} %copy-done), kind=kOutput, calls=%fused_computation.26 | convolution fusion | flops 202899456 | bytes 6299648 | tf_op jit(solution)/shard_map/pq,qmai->mapi/dot_general | solution.py:43
  407.8 9.8 %copy.62 = bf16[32,64,64,12]{1,0,3,2:T(8,128)(2,1)} copy(bf16[32,64,64,12]{2,1,3,0:T(8,128)(2,1)} %convert_bitcast_fusion.2) | data formatting | bytes 6291456 | tf_op jit(solution)/shard_map/convert_element_type | solution.py:45
  417.6 9.7 %reshape.87 = bf16[2048,768]{0,1:T(8,128)(2,1)} reshape(bf16[32,64,64,12]{1,0,3,2:T(8,128)(2,1)} %copy.62) | data formatting | bytes 6291456 | tf_op jit(solution)/shard_map/reshape | solution.py:46
  427.3 12.2 %copy.83 = bf16[64,32,768]{0,1,2:T(8,128)(2,1)} copy(bf16[64,32,768]{2,1,0:T(8,128)(2,1)} %get-tuple-element.11) | data formatting | bytes 6291456
  439.5 12.8 %convert_bitcast_fusion.1 = bf16[32,64,64,12]{2,1,3,0:T(8,128)(2,1)} fusion(bf16[64,32,64,12]{0,1,3,2:T(8,128)(2,1)} %bitcast.75, bf16[1,64,64]{2,1,0:T(8,128)(2,1)S(1)} %copy-done), kind=kOutput, calls=%fused_computation.25 | convolution fusion | flops 202899456 | bytes 6299648 | tf_op jit(solution)/shard_map/pq,qmai->mapi/dot_general | solution.py:43
  452.3 9.4 %copy.68 = bf16[32,64,64,12]{1,0,3,2:T(8,128)(2,1)} copy(bf16[32,64,64,12]{2,1,3,0:T(8,128)(2,1)} %convert_bitcast_fusion.1) | data formatting | bytes 6291456 | tf_op jit(solution)/shard_map/convert_element_type | solution.py:45
  461.7 9.9 %reshape.89 = bf16[2048,768]{0,1:T(8,128)(2,1)} reshape(bf16[32,64,64,12]{1,0,3,2:T(8,128)(2,1)} %copy.68) | data formatting | bytes 6291456 | tf_op jit(solution)/shard_map/reshape | solution.py:46
  471.6 12.2 %copy.81 = bf16[64,32,768]{0,1,2:T(8,128)(2,1)} copy(bf16[64,32,768]{2,1,0:T(8,128)(2,1)} %get-tuple-element.13) | data formatting | bytes 6291456
  483.8 12.8 %convert_bitcast_fusion.3 = bf16[32,64,64,12]{2,1,3,0:T(8,128)(2,1)} fusion(bf16[64,32,64,12]{0,1,3,2:T(8,128)(2,1)} %bitcast.76, bf16[1,64,64]{2,1,0:T(8,128)(2,1)S(1)} %copy-done), kind=kOutput, calls=%fused_computation.27 | convolution fusion | flops 202899456 | bytes 6299648 | tf_op jit(solution)/shard_map/pq,qmai->mapi/dot_general | solution.py:43
  496.6 9.4 %copy.56 = bf16[32,64,64,12]{1,0,3,2:T(8,128)(2,1)} copy(bf16[32,64,64,12]{2,1,3,0:T(8,128)(2,1)} %convert_bitcast_fusion.3) | data formatting | bytes 6291456 | tf_op jit(solution)/shard_map/convert_element_type | solution.py:45
  506.0 9.9 %reshape.85 = bf16[2048,768]{0,1:T(8,128)(2,1)} reshape(bf16[32,64,64,12]{1,0,3,2:T(8,128)(2,1)} %copy.56) | data formatting | bytes 6291456 | tf_op jit(solution)/shard_map/reshape | solution.py:46
  524.5 30.1 %reduce-scatter.2.cloned.1.call-done = f32[512,256]{1,0:T(8,128)} async-done(((f32[2048,256]{1,0:T(8,128)}), f32[512,256]{1,0:T(8,128)}) %reduce-scatter.2.cloned.1.call-update) | async-done | bytes 524304 | tf_op jit(solution)/shard_map/reduce_scatter | solution.py:50
  (151 shorter events, 171.2 us)
Async XLA Ops:
  6.5 339.5 %copy-start = (bf16[1,64,64]{2,1,0:T(8,128)(2,1)S(1)}, bf16[1,64,64]{2,1,0:T(8,128)(2,1)}, u32[]{:S(2)}) copy-start(bf16[1,64,64]{2,1,0:T(8,128)(2,1)} %param.9) | copy-start | bytes 24580
  6.5 548.0 %reduce-scatter.2.cloned.1.call-start = ((), (), s32[]{:S(2)}) async-start(), calls=%async_computation.1 | async-start | bytes 2621440 | tf_op jit(solution)/shard_map/reduce_scatter | solution.py:50
  78.6 24.6 %collective-permute-start = (bf16[8,32,768]{2,1,0:T(8,128)(2,1)}, bf16[8,32,768]{2,1,0:T(8,128)(2,1)}, u32[]{:S(2)}, u32[]{:S(2)}) collective-permute-start(bf16[8,32,768]{2,1,0:T(8,128)(2,1)} %copy.52), channel_id=1, source_target_pairs={{0,4},{4,8},{8,12},{12,16},{16,20},{20,24},{24,28},{28,0},{1,5},{5... | collective-permute-start | bytes 1179656 | tf_op jit(solution)/shard_map/ppermute | solution.py:37
  87.9 16.8 %collective-permute-start.21 = (bf16[8,32,768]{2,1,0:T(8,128)(2,1)S(1)}, bf16[8,32,768]{2,1,0:T(8,128)(2,1)}, u32[]{:S(2)}, u32[]{:S(2)}) collective-permute-start(bf16[8,32,768]{2,1,0:T(8,128)(2,1)S(1)} %copy.70), channel_id=1, source_target_pairs={{0,4},{4,8},{8,12},{12,16},{16,20},{20,24},{24,28},{28,0},{1,5},{5... | collective-permute-start | bytes 1179656 | tf_op jit(solution)/shard_map/ppermute | solution.py:37
  95.4 16.7 %collective-permute-start.14 = (bf16[8,32,768]{2,1,0:T(8,128)(2,1)S(1)}, bf16[8,32,768]{2,1,0:T(8,128)(2,1)}, u32[]{:S(2)}, u32[]{:S(2)}) collective-permute-start(bf16[8,32,768]{2,1,0:T(8,128)(2,1)S(1)} %copy.64), channel_id=1, source_target_pairs={{0,4},{4,8},{8,12},{12,16},{16,20},{20,24},{24,28},{28,0},{1,5},{5... | collective-permute-start | bytes 1179656 | tf_op jit(solution)/shard_map/ppermute | solution.py:37
  101.6 18.8 %collective-permute-start.7 = (bf16[8,32,768]{2,1,0:T(8,128)(2,1)S(1)}, bf16[8,32,768]{2,1,0:T(8,128)(2,1)S(1)}, u32[]{:S(2)}, u32[]{:S(2)}) collective-permute-start(bf16[8,32,768]{2,1,0:T(8,128)(2,1)S(1)} %copy.58), channel_id=1, source_target_pairs={{0,4},{4,8},{8,12},{12,16},{16,20},{20,24},{24,28},{28,0},{1,5},{5... | collective-permute-start | bytes 1179656 | tf_op jit(solution)/shard_map/ppermute | solution.py:37
  103.2 25.6 %collective-permute-start.1 = (bf16[8,32,768]{2,1,0:T(8,128)(2,1)}, bf16[8,32,768]{2,1,0:T(8,128)(2,1)S(1)}, u32[]{:S(2)}, u32[]{:S(2)}) collective-permute-start(bf16[8,32,768]{2,1,0:T(8,128)(2,1)} %collective-permute-done), channel_id=1, source_target_pairs={{0,4},{4,8},{8,12},{12,16},{16,20},{20,24},{24,28},{28,0},{1,5},{5... | collective-permute-start | bytes 1179656 | tf_op jit(solution)/shard_map/ppermute | solution.py:37
  104.7 32.6 %collective-permute-start.22 = (bf16[8,32,768]{2,1,0:T(8,128)(2,1)}, bf16[8,32,768]{2,1,0:T(8,128)(2,1)S(1)}, u32[]{:S(2)}, u32[]{:S(2)}) collective-permute-start(bf16[8,32,768]{2,1,0:T(8,128)(2,1)} %collective-permute-done.21), channel_id=1, source_target_pairs={{0,4},{4,8},{8,12},{12,16},{16,20},{20,24},{24,28},{28,0},{1,5},{5... | collective-permute-start | bytes 1179656 | tf_op jit(solution)/shard_map/ppermute | solution.py:37
  112.1 33.6 %collective-permute-start.15 = (bf16[8,32,768]{2,1,0:T(8,128)(2,1)}, bf16[8,32,768]{2,1,0:T(8,128)(2,1)S(1)}, u32[]{:S(2)}, u32[]{:S(2)}) collective-permute-start(bf16[8,32,768]{2,1,0:T(8,128)(2,1)} %collective-permute-done.14), channel_id=1, source_target_pairs={{0,4},{4,8},{8,12},{12,16},{16,20},{20,24},{24,28},{28,0},{1,5},{5... | collective-permute-start | bytes 1179656 | tf_op jit(solution)/shard_map/ppermute | solution.py:37
  120.4 33.7 %collective-permute-start.8 = (bf16[8,32,768]{2,1,0:T(8,128)(2,1)S(1)}, bf16[8,32,768]{2,1,0:T(8,128)(2,1)S(1)}, u32[]{:S(2)}, u32[]{:S(2)}) collective-permute-start(bf16[8,32,768]{2,1,0:T(8,128)(2,1)S(1)} %collective-permute-done.7), channel_id=1, source_target_pairs={{0,4},{4,8},{8,12},{12,16},{16,20},{20,24},{24,28},{28,0},{1,5},{5... | collective-permute-start | bytes 1179656 | tf_op jit(solution)/shard_map/ppermute | solution.py:37
  128.8 33.7 %collective-permute-start.2 = (bf16[8,32,768]{2,1,0:T(8,128)(2,1)S(1)}, bf16[8,32,768]{2,1,0:T(8,128)(2,1)S(1)}, u32[]{:S(2)}, u32[]{:S(2)}) collective-permute-start(bf16[8,32,768]{2,1,0:T(8,128)(2,1)S(1)} %collective-permute-done.1), channel_id=1, source_target_pairs={{0,4},{4,8},{8,12},{12,16},{16,20},{20,24},{24,28},{28,0},{1,5},{5... | collective-permute-start | bytes 1179656 | tf_op jit(solution)/shard_map/ppermute | solution.py:37
  137.3 33.7 %collective-permute-start.23 = (bf16[8,32,768]{2,1,0:T(8,128)(2,1)S(1)}, bf16[8,32,768]{2,1,0:T(8,128)(2,1)S(1)}, u32[]{:S(2)}, u32[]{:S(2)}) collective-permute-start(bf16[8,32,768]{2,1,0:T(8,128)(2,1)S(1)} %collective-permute-done.22), channel_id=1, source_target_pairs={{0,4},{4,8},{8,12},{12,16},{16,20},{20,24},{24,28},{28,0},{1,5},{5... | collective-permute-start | bytes 1179656 | tf_op jit(solution)/shard_map/ppermute | solution.py:37
  145.7 33.7 %collective-permute-start.16 = (bf16[8,32,768]{2,1,0:T(8,128)(2,1)S(1)}, bf16[8,32,768]{2,1,0:T(8,128)(2,1)S(1)}, u32[]{:S(2)}, u32[]{:S(2)}) collective-permute-start(bf16[8,32,768]{2,1,0:T(8,128)(2,1)S(1)} %collective-permute-done.15), channel_id=1, source_target_pairs={{0,4},{4,8},{8,12},{12,16},{16,20},{20,24},{24,28},{28,0},{1,5},{5... | collective-permute-start | bytes 1179656 | tf_op jit(solution)/shard_map/ppermute | solution.py:37
  154.1 84.4 %copy-start.8 = (bf16[8,32,768]{2,1,0:T(8,128)(2,1)}, bf16[8,32,768]{2,1,0:T(8,128)(2,1)S(1)}, u32[]{:S(2)}) copy-start(bf16[8,32,768]{2,1,0:T(8,128)(2,1)S(1)} %collective-permute-done.8) | copy-start | bytes 1179652
  154.1 33.7 %collective-permute-start.9 = (bf16[8,32,768]{2,1,0:T(8,128)(2,1)S(1)}, bf16[8,32,768]{2,1,0:T(8,128)(2,1)S(1)}, u32[]{:S(2)}, u32[]{:S(2)}) collective-permute-start(bf16[8,32,768]{2,1,0:T(8,128)(2,1)S(1)} %collective-permute-done.8), channel_id=1, source_target_pairs={{0,4},{4,8},{8,12},{12,16},{16,20},{20,24},{24,28},{28,0},{1,5},{5... | collective-permute-start | bytes 1179656 | tf_op jit(solution)/shard_map/ppermute | solution.py:37
  162.6 92.8 %copy-start.16 = (bf16[8,32,768]{2,1,0:T(8,128)(2,1)}, bf16[8,32,768]{2,1,0:T(8,128)(2,1)S(1)}, u32[]{:S(2)}) copy-start(bf16[8,32,768]{2,1,0:T(8,128)(2,1)S(1)} %collective-permute-done.2) | copy-start | bytes 1179652
  162.6 33.7 %collective-permute-start.3 = (bf16[8,32,768]{2,1,0:T(8,128)(2,1)S(1)}, bf16[8,32,768]{2,1,0:T(8,128)(2,1)S(1)}, u32[]{:S(2)}, u32[]{:S(2)}) collective-permute-start(bf16[8,32,768]{2,1,0:T(8,128)(2,1)S(1)} %collective-permute-done.2), channel_id=1, source_target_pairs={{0,4},{4,8},{8,12},{12,16},{16,20},{20,24},{24,28},{28,0},{1,5},{5... | collective-permute-start | bytes 1179656 | tf_op jit(solution)/shard_map/ppermute | solution.py:37
  171.0 33.7 %collective-permute-start.24 = (bf16[8,32,768]{2,1,0:T(8,128)(2,1)S(1)}, bf16[8,32,768]{2,1,0:T(8,128)(2,1)S(1)}, u32[]{:S(2)}, u32[]{:S(2)}) collective-permute-start(bf16[8,32,768]{2,1,0:T(8,128)(2,1)S(1)} %collective-permute-done.23), channel_id=1, source_target_pairs={{0,4},{4,8},{8,12},{12,16},{16,20},{20,24},{24,28},{28,0},{1,5},{5... | collective-permute-start | bytes 1179656 | tf_op jit(solution)/shard_map/ppermute | solution.py:37
  179.4 33.7 %collective-permute-start.17 = (bf16[8,32,768]{2,1,0:T(8,128)(2,1)S(1)}, bf16[8,32,768]{2,1,0:T(8,128)(2,1)S(1)}, u32[]{:S(2)}, u32[]{:S(2)}) collective-permute-start(bf16[8,32,768]{2,1,0:T(8,128)(2,1)S(1)} %collective-permute-done.16), channel_id=1, source_target_pairs={{0,4},{4,8},{8,12},{12,16},{16,20},{20,24},{24,28},{28,0},{1,5},{5... | collective-permute-start | bytes 1179656 | tf_op jit(solution)/shard_map/ppermute | solution.py:37
  187.8 33.7 %collective-permute-start.10 = (bf16[8,32,768]{2,1,0:T(8,128)(2,1)S(1)}, bf16[8,32,768]{2,1,0:T(8,128)(2,1)S(1)}, u32[]{:S(2)}, u32[]{:S(2)}) collective-permute-start(bf16[8,32,768]{2,1,0:T(8,128)(2,1)S(1)} %collective-permute-done.9), channel_id=1, source_target_pairs={{0,4},{4,8},{8,12},{12,16},{16,20},{20,24},{24,28},{28,0},{1,5},{5... | collective-permute-start | bytes 1179656 | tf_op jit(solution)/shard_map/ppermute | solution.py:37
  196.3 33.7 %collective-permute-start.4 = (bf16[8,32,768]{2,1,0:T(8,128)(2,1)S(1)}, bf16[8,32,768]{2,1,0:T(8,128)(2,1)S(1)}, u32[]{:S(2)}, u32[]{:S(2)}) collective-permute-start(bf16[8,32,768]{2,1,0:T(8,128)(2,1)S(1)} %collective-permute-done.3), channel_id=1, source_target_pairs={{0,4},{4,8},{8,12},{12,16},{16,20},{20,24},{24,28},{28,0},{1,5},{5... | collective-permute-start | bytes 1179656 | tf_op jit(solution)/shard_map/ppermute | solution.py:37
  204.7 33.8 %collective-permute-start.25 = (bf16[8,32,768]{2,1,0:T(8,128)(2,1)S(1)}, bf16[8,32,768]{2,1,0:T(8,128)(2,1)}, u32[]{:S(2)}, u32[]{:S(2)}) collective-permute-start(bf16[8,32,768]{2,1,0:T(8,128)(2,1)S(1)} %collective-permute-done.24), channel_id=1, source_target_pairs={{0,4},{4,8},{8,12},{12,16},{16,20},{20,24},{24,28},{28,0},{1,5},{5... | collective-permute-start | bytes 1179656 | tf_op jit(solution)/shard_map/ppermute | solution.py:37
  213.1 33.8 %collective-permute-start.18 = (bf16[8,32,768]{2,1,0:T(8,128)(2,1)S(1)}, bf16[8,32,768]{2,1,0:T(8,128)(2,1)}, u32[]{:S(2)}, u32[]{:S(2)}) collective-permute-start(bf16[8,32,768]{2,1,0:T(8,128)(2,1)S(1)} %collective-permute-done.17), channel_id=1, source_target_pairs={{0,4},{4,8},{8,12},{12,16},{16,20},{20,24},{24,28},{28,0},{1,5},{5... | collective-permute-start | bytes 1179656 | tf_op jit(solution)/shard_map/ppermute | solution.py:37
  221.5 33.8 %collective-permute-start.11 = (bf16[8,32,768]{2,1,0:T(8,128)(2,1)S(1)}, bf16[8,32,768]{2,1,0:T(8,128)(2,1)}, u32[]{:S(2)}, u32[]{:S(2)}) collective-permute-start(bf16[8,32,768]{2,1,0:T(8,128)(2,1)S(1)} %collective-permute-done.10), channel_id=1, source_target_pairs={{0,4},{4,8},{8,12},{12,16},{16,20},{20,24},{24,28},{28,0},{1,5},{5... | collective-permute-start | bytes 1179656 | tf_op jit(solution)/shard_map/ppermute | solution.py:37
  230.0 33.8 %collective-permute-start.5 = (bf16[8,32,768]{2,1,0:T(8,128)(2,1)S(1)}, bf16[8,32,768]{2,1,0:T(8,128)(2,1)}, u32[]{:S(2)}, u32[]{:S(2)}) collective-permute-start(bf16[8,32,768]{2,1,0:T(8,128)(2,1)S(1)} %collective-permute-done.4), channel_id=1, source_target_pairs={{0,4},{4,8},{8,12},{12,16},{16,20},{20,24},{24,28},{28,0},{1,5},{5... | collective-permute-start | bytes 1179656 | tf_op jit(solution)/shard_map/ppermute | solution.py:37
  238.5 33.7 %collective-permute-start.26 = (bf16[8,32,768]{2,1,0:T(8,128)(2,1)}, bf16[8,32,768]{2,1,0:T(8,128)(2,1)}, u32[]{:S(2)}, u32[]{:S(2)}) collective-permute-start(bf16[8,32,768]{2,1,0:T(8,128)(2,1)} %collective-permute-done.25), channel_id=1, source_target_pairs={{0,4},{4,8},{8,12},{12,16},{16,20},{20,24},{24,28},{28,0},{1,5},{5... | collective-permute-start | bytes 1179656 | tf_op jit(solution)/shard_map/ppermute | solution.py:37
  246.9 33.7 %collective-permute-start.19 = (bf16[8,32,768]{2,1,0:T(8,128)(2,1)}, bf16[8,32,768]{2,1,0:T(8,128)(2,1)}, u32[]{:S(2)}, u32[]{:S(2)}) collective-permute-start(bf16[8,32,768]{2,1,0:T(8,128)(2,1)} %collective-permute-done.18), channel_id=1, source_target_pairs={{0,4},{4,8},{8,12},{12,16},{16,20},{20,24},{24,28},{28,0},{1,5},{5... | collective-permute-start | bytes 1179656 | tf_op jit(solution)/shard_map/ppermute | solution.py:37
  255.4 33.7 %collective-permute-start.12 = (bf16[8,32,768]{2,1,0:T(8,128)(2,1)}, bf16[8,32,768]{2,1,0:T(8,128)(2,1)}, u32[]{:S(2)}, u32[]{:S(2)}) collective-permute-start(bf16[8,32,768]{2,1,0:T(8,128)(2,1)} %collective-permute-done.11), channel_id=1, source_target_pairs={{0,4},{4,8},{8,12},{12,16},{16,20},{20,24},{24,28},{28,0},{1,5},{5... | collective-permute-start | bytes 1179656 | tf_op jit(solution)/shard_map/ppermute | solution.py:37
  263.8 33.7 %collective-permute-start.6 = (bf16[8,32,768]{2,1,0:T(8,128)(2,1)}, bf16[8,32,768]{2,1,0:T(8,128)(2,1)}, u32[]{:S(2)}, u32[]{:S(2)}) collective-permute-start(bf16[8,32,768]{2,1,0:T(8,128)(2,1)} %collective-permute-done.5), channel_id=1, source_target_pairs={{0,4},{4,8},{8,12},{12,16},{16,20},{20,24},{24,28},{28,0},{1,5},{5... | collective-permute-start | bytes 1179656 | tf_op jit(solution)/shard_map/ppermute | solution.py:37
  272.2 55.6 %collective-permute-start.27 = (bf16[8,32,768]{2,1,0:T(8,128)(2,1)}, bf16[8,32,768]{2,1,0:T(8,128)(2,1)S(1)}, u32[]{:S(2)}, u32[]{:S(2)}) collective-permute-start(bf16[8,32,768]{2,1,0:T(8,128)(2,1)} %collective-permute-done.26), channel_id=1, source_target_pairs={{0,4},{4,8},{8,12},{12,16},{16,20},{20,24},{24,28},{28,0},{1,5},{5... | collective-permute-start | bytes 1179656 | tf_op jit(solution)/shard_map/ppermute | solution.py:37
  280.6 43.5 %collective-permute-start.20 = (bf16[8,32,768]{2,1,0:T(8,128)(2,1)}, bf16[8,32,768]{2,1,0:T(8,128)(2,1)S(1)}, u32[]{:S(2)}, u32[]{:S(2)}) collective-permute-start(bf16[8,32,768]{2,1,0:T(8,128)(2,1)} %collective-permute-done.19), channel_id=1, source_target_pairs={{0,4},{4,8},{8,12},{12,16},{16,20},{20,24},{24,28},{28,0},{1,5},{5... | collective-permute-start | bytes 1179656 | tf_op jit(solution)/shard_map/ppermute | solution.py:37
  289.1 32.8 %collective-permute-start.13 = (bf16[8,32,768]{2,1,0:T(8,128)(2,1)}, bf16[8,32,768]{2,1,0:T(8,128)(2,1)S(1)}, u32[]{:S(2)}, u32[]{:S(2)}) collective-permute-start(bf16[8,32,768]{2,1,0:T(8,128)(2,1)} %collective-permute-done.12), channel_id=1, source_target_pairs={{0,4},{4,8},{8,12},{12,16},{16,20},{20,24},{24,28},{28,0},{1,5},{5... | collective-permute-start | bytes 1179656 | tf_op jit(solution)/shard_map/ppermute | solution.py:37
  (20 other events, 503.0 us)
Sparse Core Ops, SparseCore 0:
  524.6 29.8 reduce-scatter.1
